TPU v7x, 128 devices: a whole 4x4x4 slice. The times are simulated.
128 devices in a mesh: rep: 4 (over z), shard: 32 (over x, y, core).
Axes of the slice: x: 4, y: 4, z: 4, core: 2. Of those that a mesh axis runs over, the one named last changes fastest.
Arguments:
- trained_sq: float32 [4, 4, 768, 768], P('rep', None, 'shard'), may hold values from -6 to 6
- trained_up: float32 [4, 768, 3072], P('rep', 'shard'), may hold values from -6 to 6
- trained_down: float32 [4, 3072, 768], P('rep', 'shard'), may hold values from -6 to 6
- trained_ln: float32 [4, 4, 768], P('rep', None, 'shard'), may hold values from -6 to 6
- start_sq: float32 [4, 768, 768], P(None, 'shard'), may hold values from -6 to 6
- start_up: float32 [768, 3072], P('shard'), may hold values from -6 to 6
- start_down: float32 [3072, 768], P('shard'), may hold values from -6 to 6
- start_ln: float32 [4, 768], P(None, 'shard'), may hold values from -6 to 6
- resid_sq: float32 [4, 4, 768, 768], P('rep', None, 'shard'), may hold values from -4 to 4
- resid_up: float32 [4, 768, 3072], P('rep', 'shard'), may hold values from -4 to 4
- resid_down: float32 [4, 3072, 768], P('rep', 'shard'), may hold values from -4 to 4
- mom_sq: float32 [4, 768, 768], P(None, 'shard'), may hold values from -3 to 3
- mom_up: float32 [768, 3072], P('shard'), may hold values from -3 to 3
- mom_down: float32 [3072, 768], P('shard'), may hold values from -3 to 3
- mom_ln: float32 [4, 768], P(None, 'shard'), may hold values from -3 to 3
- basis_sq: float32 [4, 768, 64], replicated, may hold values from -0.21875 to 0.21875
- basis_up: float32 [3072, 64], replicated, may hold values from -0.109375 to 0.109375
- basis_down: float32 [768, 64], replicated, may hold values from -0.21875 to 0.21875
Outputs:
- new_resid_sq: float32 [4, 4, 768, 768], P('rep', None, 'shard')
- new_resid_up: float32 [4, 768, 3072], P('rep', 'shard')
- new_resid_down: float32 [4, 3072, 768], P('rep', 'shard')
- new_mom_sq: float32 [4, 768, 768], P(None, 'shard')
- new_mom_up: float32 [768, 3072], P('shard')
- new_mom_down: float32 [3072, 768], P('shard')
- new_mom_ln: float32 [4, 768], P(None, 'shard')
- weights_sq: bfloat16 [4, 768, 768], replicated
- weights_up: bfloat16 [768, 3072], replicated
- weights_down: bfloat16 [3072, 768], replicated
- weights_ln: bfloat16 [4, 768], replicated
All inputs are finite; a program needn't handle non-finite values.
Results may differ from a plain program's by a relative error of at most 0.001.
Values may be sent and summed in bfloat16 or wider, within the bound.
No kernel may reach another device: no remote copies, remote signals or barrier semaphores. Data moves between devices by JAX's collectives and lax.ppermute only.
A program may use at most 128 MiB of HBM per device.

v0:
```python
import jax
import jax.numpy as jnp
from jax import lax
from jax.sharding import PartitionSpec as P

moment_coef = 0.9
outer_rate = 0.7


def advance(start, moment, outer):
    new_moment = moment_coef * moment + outer
    weights = (start - outer_rate * (outer + moment_coef * new_moment)).astype(jnp.bfloat16)
    return (new_moment, weights)


def on_device(
    trained_sq,
    trained_up,
    trained_down,
    trained_ln,
    start_sq,
    start_up,
    start_down,
    start_ln,
    resid_sq,
    resid_up,
    resid_down,
    mom_sq,
    mom_up,
    mom_down,
    mom_ln,
    basis_sq,
    basis_up,
    basis_down,
):
    highest = lax.Precision.HIGHEST
    groups = lax.axis_size("rep")
    delta_sq = start_sq - trained_sq[0] + resid_sq[0]
    factor_sq = jnp.einsum("mrd,mdk->mrk", delta_sq, basis_sq, precision=highest)
    new_resid_sq = delta_sq - jnp.einsum("mrk,mdk->mrd", factor_sq, basis_sq, precision=highest)
    delta_up = start_up - trained_up[0] + resid_up[0]
    factor_up = jnp.dot(delta_up, basis_up, precision=highest, preferred_element_type=jnp.float32)
    new_resid_up = delta_up - jnp.einsum("rk,fk->rf", factor_up, basis_up, precision=highest)
    delta_down = start_down - trained_down[0] + resid_down[0]
    factor_down = jnp.dot(
        delta_down, basis_down, precision=highest, preferred_element_type=jnp.float32
    )
    new_resid_down = delta_down - jnp.einsum(
        "rk,dk->rd", factor_down, basis_down, precision=highest
    )
    norm_delta = start_ln - trained_ln[0]
    summed = lax.psum((factor_sq, factor_up, factor_down, norm_delta), "rep")
    mean_sq = summed[0] / groups
    mean_up = summed[1] / groups
    mean_down = summed[2] / groups
    mean_ln = summed[3] / groups
    new_mom_ln, norm_weights = advance(start_ln, mom_ln, mean_ln)
    outer_sq = jnp.einsum("mrk,mdk->mrd", mean_sq, basis_sq, precision=highest)
    outer_up = jnp.einsum("rk,fk->rf", mean_up, basis_up, precision=highest)
    outer_down = jnp.einsum("rk,dk->rd", mean_down, basis_down, precision=highest)
    new_mom_sq, owned_sq = advance(start_sq, mom_sq, outer_sq)
    new_mom_up, owned_up = advance(start_up, mom_up, outer_up)
    new_mom_down, owned_down = advance(start_down, mom_down, outer_down)
    weights_sq, weights_up, weights_down, weights_ln = (
        lax.all_gather(owned_sq, "shard", axis=1, tiled=True),
        lax.all_gather(owned_up, "shard", axis=0, tiled=True),
        lax.all_gather(owned_down, "shard", axis=0, tiled=True),
        lax.all_gather(norm_weights, "shard", axis=1, tiled=True),
    )
    return (
        new_resid_sq[None],
        new_resid_up[None],
        new_resid_down[None],
        new_mom_sq,
        new_mom_up,
        new_mom_down,
        new_mom_ln,
        weights_sq,
        weights_up,
        weights_down,
        weights_ln,
    )


def solution(mesh):
    placed = (
        P("rep", None, "shard", None),
        P("rep", "shard", None),
        P("rep", "shard", None),
        P("rep", None, "shard"),
        P(None, "shard", None),
        P("shard", None),
        P("shard", None),
        P(None, "shard"),
        P("rep", None, "shard", None),
        P("rep", "shard", None),
        P("rep", "shard", None),
        P(None, "shard", None),
        P("shard", None),
        P("shard", None),
        P(None, "shard"),
        P(),
        P(),
        P(),
    )
    return jax.shard_map(
        on_device,
        mesh=mesh,
        in_specs=placed,
        out_specs=(
            P("rep", None, "shard", None),
            P("rep", "shard", None),
            P("rep", "shard", None),
            P(None, "shard", None),
            P("shard", None),
            P("shard", None),
            P(None, "shard"),
            P(),
            P(),
            P(),
            P(),
        ),
        check_vma=False,
    )
```

profile of v0, /device:TPU:1, one launch (start us, length us, event | category | flops | bytes accessed | tf_op | source)
XLA Modules:
  0.0 201.4 jit_solution(2891028444277751555)
XLA Ops:
  7.3 0.9 bitcast_subtract_fusion.3
  8.2 0.5 copy-done
  8.7 2.6 %fusion.16 = f32[4,24,64]{2,1,0:T(8,128)} fusion(f32[4,768,64]{1,2,0:T(8,128)S(1)} %copy-done, f32[1,4,24,768]{3,2,1,0:T(8,128)} %param.26, f32[4,24,768]{2,1,0:T(8,128)} %param.22, f32[1,4,24,768]{3,2,1,0:T(8,128)} %param.18), kind=kOutput, calls=%fused_computation.34 | convolution fusion | flops 56770560 | bytes 1695744 | tf_op jit(solution)/shard_map/mrd,mdk->mrk/dot_general | solution.py:39
  11.2 2.3 %fusion.18 = f32[96,64]{0,1:T(8,128)} fusion(f32[768,64]{0,1:T(8,128)} %param.35, f32[1,96,768]{2,1,0:T(8,128)} %param.28, f32[96,768]{1,0:T(8,128)} %param.24, f32[1,96,768]{2,1,0:T(8,128)} %param.20), kind=kOutput, calls=%fused_computation.36 | convolution fusion | flops 56770560 | bytes 1105920 | tf_op jit(solution)/shard_map/dot_general | solution.py:45
  13.5 2.1 %fusion.17 = f32[24,64]{1,0:T(8,128)S(1)} fusion(f32[3072,64]{0,1:T(8,128)} %param.34, f32[1,24,3072]{2,1,0:T(8,128)} %param.27, f32[24,3072]{1,0:T(8,128)} %param.23, f32[1,24,3072]{2,1,0:T(8,128)} %param.19), kind=kOutput, calls=%fused_computation.35 | convolution fusion | flops 56770560 | bytes 1677312 | tf_op jit(solution)/shard_map/dot_general | solution.py:42
  15.6 17.3 %all-reduce = (f32[4,24,64]{2,1,0:T(8,128)}, f32[24,64]{1,0:T(8,128)}, f32[96,64]{0,1:T(8,128)}, f32[4,24]{1,0:T(4,128)}) all-reduce(f32[4,24,64]{2,1,0:T(8,128)} %fusion.16, f32[24,64]{1,0:T(8,128)S(1)} %fusion.17, f32[96,64]{0,1:T(8,128)} %fusion.18, f32[4,24]{1,0:T(4,128)S(1)} %bitcast_subtract_fusion.3), channel_id=1, replica_groups=mesh['rep'=4,'shard'=32] {'rep'}, use_global_device_ids=true, to_apply=%region_0.0 | all-reduce | flops 13920 | bytes 111360 | tf_op jit(solution)/shard_map/psum | solution.py:52
  33.0 2.3 %subtract_convert_fusion.2 = (bf16[4,24,768]{2,1,0:T(8,128)(2,1)}, f32[4,24,768]{2,1,0:T(8,128)}) fusion(f32[4,24,768]{2,1,0:T(8,128)S(1)} %copy-done.5, f32[4,24,768]{2,1,0:T(8,128)} %param.29, f32[4,768,64]{1,2,0:T(8,128)S(1)} %copy-done, f32[4,24,64]{2,1,0:T(8,128)} %get-tuple-element.11), kind=kOutput, calls=%fused_computation.14 | convolution fusion | flops 57145344 | bytes 1843200 | tf_op jit(solution)/shard_map/mrk,mdk->mrd/dot_general | solution.py:58
  35.4 2.3 %subtract_convert_fusion.1 = (bf16[24,3072]{1,0:T(8,128)(2,1)}, f32[24,3072]{1,0:T(8,128)}) fusion(f32[24,3072]{1,0:T(8,128)S(1)} %copy-done.3, f32[24,3072]{1,0:T(8,128)} %param.30, f32[3072,64]{0,1:T(8,128)S(1)} %copy-done.1, f32[24,64]{1,0:T(8,128)} %get-tuple-element.12), kind=kOutput, calls=%fused_computation.13 | convolution fusion | flops 57140736 | bytes 1824768 | tf_op jit(solution)/shard_map/rk,fk->rf/dot_general | solution.py:59
  37.7 2.2 %subtract_convert_fusion = (bf16[96,768]{1,0:T(8,128)(2,1)}, f32[96,768]{1,0:T(8,128)}) fusion(f32[96,768]{1,0:T(8,128)S(1)} %copy-done.4, f32[96,768]{1,0:T(8,128)} %param.31, f32[768,64]{0,1:T(8,128)S(1)} %copy-done.6, f32[96,64]{0,1:T(8,128)} %get-tuple-element.13), kind=kOutput, calls=%fused_computation.12 | convolution fusion | flops 57145344 | bytes 1253376 | tf_op jit(solution)/shard_map/rk,dk->rd/dot_general | solution.py:60
  40.0 1.3 fusion.12
  41.3 28.7 %all-gather = bf16[32,24,4]{1,2,0:T(4,128)(2,1)S(1)} all-gather(bf16[1,24,4]{1,2,0:T(4,128)(2,1)S(1)} %get-tuple-element.15), channel_id=1, replica_groups=mesh['rep'=4,'shard'=32] {'shard'}, dimensions={0}, use_global_device_ids=true | all-gather | bytes 6336 | tf_op jit(solution)/shard_map/all_gather | solution.py:68
  69.9 0.6 copy.30
  70.6 1.5 reshape.23
  72.0 2.1 %fusion.1 = f32[1,96,768]{2,1,0:T(8,128)} fusion(f32[96,64]{0,1:T(8,128)} %fusion.18, f32[768,64]{0,1:T(8,128)S(1)} %copy-done.6, f32[1,96,768]{2,1,0:T(8,128)S(1)} %copy-done.9, f32[96,768]{1,0:T(8,128)S(1)} %copy-done.4, f32[1,96,768]{2,1,0:T(8,128)} %param.20), kind=kOutput, calls=%fused_computation.3 | convolution fusion | flops 56844288 | bytes 1400832 | tf_op jit(solution)/shard_map/rk,dk->rd/dot_general | solution.py:48
  74.2 1.2 fusion
  75.4 2.3 %fusion.2 = f32[1,4,24,768]{3,2,1,0:T(8,128)} fusion(f32[4,24,64]{2,1,0:T(8,128)} %fusion.16, f32[4,768,64]{1,2,0:T(8,128)S(1)} %copy-done, f32[1,4,24,768]{3,2,1,0:T(8,128)} %param.26, f32[4,24,768]{2,1,0:T(8,128)S(1)} %copy-done.5, f32[1,4,24,768]{3,2,1,0:T(8,128)} %param.18), kind=kOutput, calls=%fused_computation.5 | convolution fusion | flops 56844288 | bytes 1990656 | tf_op jit(solution)/shard_map/mrk,mdk->mrd/dot_general | solution.py:40
  77.7 8.5 %all-gather.5.cloned.1.call-done = bf16[4,768,768]{2,1,0:T(8,128)(2,1)} async-done(((bf16[4,24,768]{2,1,0:T(8,128)(2,1)}), bf16[4,768,768]{2,1,0:T(8,128)(2,1)}) %all-gather.5.cloned.1.call-update) | async-done | bytes 4718608 | tf_op jit(solution)/shard_map/all_gather | solution.py:65
  86.2 49.0 %all-gather.7.cloned.1.call-done = bf16[768,3072]{1,0:T(8,128)(2,1)} async-done(((bf16[24,3072]{1,0:T(8,128)(2,1)}), bf16[768,3072]{1,0:T(8,128)(2,1)}) %all-gather.7.cloned.1.call-update) | async-done | bytes 4718608 | tf_op jit(solution)/shard_map/all_gather | solution.py:66
  135.1 49.0 %all-gather.9.cloned.1.call-done = bf16[3072,768]{1,0:T(8,128)(2,1)} async-done(((bf16[96,768]{1,0:T(8,128)(2,1)}), bf16[3072,768]{1,0:T(8,128)(2,1)}) %all-gather.9.cloned.1.call-update) | async-done | bytes 4718608 | tf_op jit(solution)/shard_map/all_gather | solution.py:67
  184.1 5.2 %copy.34 = bf16[4,768,768]{2,1,0:T(8,128)(2,1)} copy(bf16[4,768,768]{2,1,0:T(8,128)(2,1)} %all-gather.5.cloned.1.call-done) | data formatting | bytes 9437184
  189.3 2.4 %copy.35 = bf16[768,3072]{1,0:T(8,128)(2,1)} copy(bf16[768,3072]{1,0:T(8,128)(2,1)S(1)} %copy-done.2) | data formatting | bytes 9437184
  191.7 0.5 slice-done
  192.2 0.5 slice-done.1
  192.7 2.2 %copy.36 = bf16[3072,768]{1,0:T(8,128)(2,1)} copy(bf16[3072,768]{1,0:T(8,128)(2,1)S(1)} %bitcast.64) | data formatting | bytes 9437184
  (30 shorter events, 0.2 us)
Async XLA Ops:
  7.2 1.5 copy-start
  7.2 25.8 %copy-start.5 = (f32[4,24,768]{2,1,0:T(8,128)S(1)}, f32[4,24,768]{2,1,0:T(8,128)}, u32[]{:S(2)}) copy-start(f32[4,24,768]{2,1,0:T(8,128)} %param.22) | copy-start | bytes 884740
  7.2 30.5 %copy-start.4 = (f32[96,768]{1,0:T(8,128)S(1)}, f32[96,768]{1,0:T(8,128)}, u32[]{:S(2)}) copy-start(f32[96,768]{1,0:T(8,128)} %param.24) | copy-start | bytes 884740
  7.2 30.5 %copy-start.6 = (f32[768,64]{0,1:T(8,128)S(1)}, f32[768,64]{0,1:T(8,128)}, u32[]{:S(2)}) copy-start(f32[768,64]{0,1:T(8,128)} %param.35) | copy-start | bytes 589828
  7.2 28.1 %copy-start.3 = (f32[24,3072]{1,0:T(8,128)S(1)}, f32[24,3072]{1,0:T(8,128)}, u32[]{:S(2)}) copy-start(f32[24,3072]{1,0:T(8,128)} %param.23) | copy-start | bytes 884740
  7.2 28.1 %copy-start.1 = (f32[3072,64]{0,1:T(8,128)S(1)}, f32[3072,64]{0,1:T(8,128)}, u32[]{:S(2)}) copy-start(f32[3072,64]{0,1:T(8,128)} %param.34) | copy-start | bytes 2359300
  7.3 78.9 %all-gather.5.cloned.1.call-start = ((), (), s32[]{:S(2)}) async-start(), calls=%async_computation | async-start | bytes 4866048 | tf_op jit(solution)/shard_map/all_gather | solution.py:65
  8.7 63.3 %copy-start.9 = (f32[1,96,768]{2,1,0:T(8,128)S(1)}, f32[1,96,768]{2,1,0:T(8,128)}, u32[]{:S(2)}) copy-start(f32[1,96,768]{2,1,0:T(8,128)} %param.28) | copy-start | bytes 884740
  11.2 62.9 %copy-start.7 = (f32[1,24,3072]{2,1,0:T(8,128)S(1)}, f32[1,24,3072]{2,1,0:T(8,128)}, u32[]{:S(2)}) copy-start(f32[1,24,3072]{2,1,0:T(8,128)} %param.27) | copy-start | bytes 884740
  11.2 62.9 %copy-start.8 = (f32[1,24,3072]{2,1,0:T(8,128)S(1)}, f32[1,24,3072]{2,1,0:T(8,128)}, u32[]{:S(2)}) copy-start(f32[1,24,3072]{2,1,0:T(8,128)} %param.19) | copy-start | bytes 884740
  33.0 7.0 %copy-start.10 = (f32[4,24]{1,0:T(4,128)S(1)}, f32[4,24]{1,0:T(4,128)}, u32[]{:S(2)}) copy-start(f32[4,24]{1,0:T(4,128)} %get-tuple-element.14) | copy-start | bytes 1156
  35.3 99.8 %all-gather.7.cloned.1.call-start = ((), (), s32[]{:S(2)}) async-start(), calls=%async_computation.1 | async-start | bytes 4866048 | tf_op jit(solution)/shard_map/all_gather | solution.py:66
  37.6 146.5 %all-gather.9.cloned.1.call-start = ((), (), s32[]{:S(2)}) async-start(), calls=%async_computation.2 | async-start | bytes 4866048 | tf_op jit(solution)/shard_map/all_gather | solution.py:67
  184.1 5.2 %copy-start.2 = (bf16[768,3072]{1,0:T(8,128)(2,1)S(1)}, bf16[768,3072]{1,0:T(8,128)(2,1)}, u32[]{:S(2)}) copy-start(bf16[768,3072]{1,0:T(8,128)(2,1)} %all-gather.7.cloned.1.call-done) | copy-start | bytes 14155780
  184.1 8.0 %slice-start = ((s8[4718592]{0:T(1024)(128)(4,1)}), s8[4194304]{0:T(1024)(128)(4,1)S(1)}, s32[]{:S(2)}) async-start(s8[4718592]{0:T(1024)(128)(4,1)} %bitcast.63), calls=%async_computation.3 | async-start | bytes 8388608
  189.3 3.4 %slice-start.1 = ((s8[4718592]{0:T(1024)(128)(4,1)}), s8[524288]{0:T(1024)(128)(4,1)S(1)}, s32[]{:S(2)}) async-start(s8[4718592]{0:T(1024)(128)(4,1)} %bitcast.63), calls=%async_computation.4 | async-start | bytes 1048576
Sparse Core Ops, SparseCore 0:
  35.4 50.7 all-gather.4
  89.0 46.0 all-gather.6
  137.9 46.1 all-gather.8
where the time goes:
time: 202 us; the launch traced here: 201 us
  waiting for transfers between devices  106 us (52%)
  blocking collectives  46 us (23%)
  matrix products  19.4 us (10%)
  between operations  13.9 us (7%)
  local copies, waits for them, and re-layouts  13.4 us (7%)
  other arithmetic  2.13 us (1%)
    all_gather x1, waiting for transfers between devices, on_device(): lax.all_gather(owned_down, 'shard', axis=0, tiled=True)  49 us
    all_gather x1, waiting for transfers between devices, on_device(): lax.all_gather(owned_up, 'shard', axis=0, tiled=True)  49 us
    all_gather x1, blocking collectives, on_device(): lax.all_gather(norm_weights, 'shard', axis=1, tiled=True)  28.7 us
    psum x1, blocking collectives, on_device(): summed = lax.psum((factor_sq, factor_up, factor_down, norm_delta), 'rep')  17.3 us
    unnamed x30, local copies, waits for them, and re-layouts  12.8 us
    all_gather x1, waiting for transfers between devices, on_device(): lax.all_gather(owned_sq, 'shard', axis=1, tiled=True)  8.47 us
  transfers between devices with their start and end apart: 3, of which 3 were waited for; matrix products, arithmetic and copies ran while one was open for 7% of the time, Pallas kernels for 0%

commit v1 on v0

--- a/solution.py
+++ b/solution.py
@@ -64,7 +64,9 @@
     weights_sq, weights_up, weights_down, weights_ln = (
         lax.all_gather(owned_sq, "shard", axis=1, tiled=True),
         lax.all_gather(owned_up, "shard", axis=0, tiled=True),
-        lax.all_gather(owned_down, "shard", axis=0, tiled=True),
+        jnp.concatenate(
+            lax.all_to_all(jnp.stack([owned_down] * lax.axis_size("shard")), "shard", 0, 0), axis=0
+        ),
         lax.all_gather(norm_weights, "shard", axis=1, tiled=True),
     )
     return (

time: 202 us -> 190 us (0.941)
  waiting for transfers between devices: 106 us -> 28 us
  blocking collectives: 46 us -> 99.7 us
  starting transfers between devices: 0.12 us -> 11.8 us
  local copies, waits for them, and re-layouts: 13.4 us -> 17.5 us
  matrix products: 19.4 us -> 16 us
    all_gather x1, blocking collectives: 28.7 us -> 82.9 us  [on_device(): lax.all_gather(norm_weights, 'shard', axis=1, tiled=True)]
    all_gather x1 -> x0, waiting for transfers between devices: 49 us -> none  [on_device(): lax.all_gather(owned_down, 'shard', axis=0, tiled=True)]
    all_gather x1, waiting for transfers between devices: 49 us -> 27.9 us  [on_device(): lax.all_gather(owned_up, 'shard', axis=0, tiled=True)]
    all_to_all x0 -> x1, starting transfers between devices: none -> 11.7 us  [on_device(): lax.all_to_all(jnp.stack([owned_down] * lax.axis_size('shard')), 'shard',...]
    all_gather x1, waiting for transfers between devices: 8.47 us -> 0.01 us  [on_device(): lax.all_gather(owned_sq, 'shard', axis=1, tiled=True)]
    another operation x0 -> x1, local copies, waits for them, and re-layouts: none -> 2.72 us  [on_device(): jnp.stack([owned_down] * lax.axis_size('shard'))]
    unnamed x30 -> x34, local copies, waits for them, and re-layouts: 12.8 us -> 14.2 us
  transfers between devices with their start and end apart: 3 -> 3, of which waited for: 3 -> 1; matrix products, arithmetic and copies ran while one was open for 7% -> 8% of each run, Pallas kernels for 0% -> 0%
where the time goes in v1:
time: 190 us; the launch traced here: 189 us
  blocking collectives  99.7 us (52%)
  waiting for transfers between devices  28 us (15%)
  local copies, waits for them, and re-layouts  17.5 us (9%)
  matrix products  16 us (8%)
  between operations  14.2 us (7%)
  starting transfers between devices  11.8 us (6%)
  other arithmetic  2.14 us (1%)
    all_gather x1, blocking collectives, on_device(): lax.all_gather(norm_weights, 'shard', axis=1, tiled=True)  82.9 us
    all_gather x1, waiting for transfers between devices, on_device(): lax.all_gather(owned_up, 'shard', axis=0, tiled=True)  27.9 us
    psum x1, blocking collectives, on_device(): summed = lax.psum((factor_sq, factor_up, factor_down, norm_delta), 'rep')  16.8 us
    unnamed x34, local copies, waits for them, and re-layouts  14.2 us
    all_to_all x1, starting transfers between devices, on_device(): lax.all_to_all(jnp.stack([owned_down] * lax.axis_size('shard')), 'shard',...  11.7 us
  transfers between devices with their start and end apart: 3, of which 1 were waited for; matrix products, arithmetic and copies ran while one was open for 8% of the time, Pallas kernels for 0%

profile of v1, /device:TPU:1, one launch (start us, length us, event | category | flops | bytes accessed | tf_op | source)
XLA Modules:
  0.0 189.4 jit_solution(17082023390325959224)
XLA Ops:
  7.3 0.0 all-gather.4.cloned.1.call-start
  7.3 0.9 bitcast_subtract_fusion.3
  8.2 0.6 copy-done
  8.8 1.9 %fusion.16 = f32[4,24,64]{2,1,0:T(8,128)S(1)} fusion(f32[4,768,64]{1,2,0:T(8,128)S(1)} %copy-done, f32[1,4,24,768]{3,2,1,0:T(8,128)} %param.26, f32[4,24,768]{2,1,0:T(8,128)} %param.22, f32[1,4,24,768]{3,2,1,0:T(8,128)} %param.18), kind=kOutput, calls=%fused_computation.34 | convolution fusion | flops 56770560 | bytes 1695744 | tf_op jit(solution)/shard_map/mrd,mdk->mrk/dot_general | solution.py:39
  10.7 1.6 fusion.18
  12.4 2.1 %fusion.17 = f32[24,64]{1,0:T(8,128)S(1)} fusion(f32[3072,64]{0,1:T(8,128)} %param.34, f32[1,24,3072]{2,1,0:T(8,128)} %param.27, f32[24,3072]{1,0:T(8,128)} %param.23, f32[1,24,3072]{2,1,0:T(8,128)} %param.19), kind=kOutput, calls=%fused_computation.35 | convolution fusion | flops 56770560 | bytes 1677312 | tf_op jit(solution)/shard_map/dot_general | solution.py:42
  14.5 16.8 %all-reduce = (f32[4,24,64]{2,1,0:T(8,128)S(1)}, f32[24,64]{1,0:T(8,128)S(1)}, f32[96,64]{0,1:T(8,128)S(1)}, f32[4,24]{1,0:T(4,128)}) all-reduce(f32[4,24,64]{2,1,0:T(8,128)S(1)} %fusion.16, f32[24,64]{1,0:T(8,128)S(1)} %fusion.17, f32[96,64]{0,1:T(8,128)S(1)} %fusion.18, ...), channel_id=1, replica_groups=mesh['rep'=4,'shard'=32] {'rep'}, use_global_device_ids=true, to_apply=%region_0.0 | all-reduce | flops 13920 | bytes 111360 | tf_op jit(solution)/shard_map/psum | solution.py:52
  31.3 1.3 subtract_convert_fusion.2
  32.6 0.0 all-gather.6.cloned.1.call-start
  32.7 1.3 subtract_convert_fusion.1
  34.1 2.2 %subtract_convert_fusion = (bf16[96,768]{1,0:T(8,128)(2,1)S(1)}, f32[96,768]{1,0:T(8,128)}) fusion(f32[96,768]{1,0:T(8,128)S(1)} %copy-done.4, f32[96,768]{1,0:T(8,128)} %param.31, f32[768,64]{0,1:T(8,128)S(1)} %copy-done.6, f32[96,64]{0,1:T(8,128)S(1)} %get-tuple-element.13), kind=kOutput, calls=%fused_computation.12 | convolution fusion | flops 57145344 | bytes 1253376 | tf_op jit(solution)/shard_map/rk,dk->rd/dot_general | solution.py:60
  36.2 2.7 %stack.2 = bf16[32,96,768]{2,1,0:T(8,128)(2,1)} broadcast(bf16[96,768]{1,0:T(8,128)(2,1)S(1)} %get-tuple-element.17), dimensions={1,2} | broadcast | bytes 4866048 | tf_op jit(solution)/shard_map/stack | solution.py:68
  39.0 11.7 %all-to-all-start = ((bf16[32,96,768]{2,1,0:T(8,128)(2,1)}), bf16[32,96,768]{2,1,0:T(8,128)(2,1)}, u32[]{:S(2)}, u32[]{:S(2)}) async-start(bf16[32,96,768]{2,1,0:T(8,128)(2,1)} %stack.2), calls=%async_computation | async-start | bytes 9437184 | tf_op jit(solution)/shard_map/all_to_all | solution.py:68
  50.7 1.3 fusion.12
  52.0 82.9 %all-gather = bf16[32,24,4]{1,2,0:T(4,128)(2,1)S(1)} all-gather(bf16[1,24,4]{1,2,0:T(4,128)(2,1)S(1)} %get-tuple-element.15), channel_id=1, replica_groups=mesh['rep'=4,'shard'=32] {'shard'}, dimensions={0}, use_global_device_ids=true | all-gather | bytes 6336 | tf_op jit(solution)/shard_map/all_gather | solution.py:70
  134.9 0.6 copy.30
  135.5 1.5 reshape.29
  137.0 2.1 %fusion.1 = f32[1,96,768]{2,1,0:T(8,128)} fusion(f32[96,64]{0,1:T(8,128)} %copy-done.13, f32[768,64]{0,1:T(8,128)S(1)} %copy-done.6, f32[1,96,768]{2,1,0:T(8,128)S(1)} %copy-done.9, f32[96,768]{1,0:T(8,128)S(1)} %copy-done.4, f32[1,96,768]{2,1,0:T(8,128)} %param.20), kind=kOutput, calls=%fused_computation.3 | convolution fusion | flops 56844288 | bytes 1400832 | tf_op jit(solution)/shard_map/rk,dk->rd/dot_general | solution.py:48
  139.1 1.2 fusion
  140.3 2.3 %fusion.2 = f32[1,4,24,768]{3,2,1,0:T(8,128)} fusion(f32[4,24,64]{2,1,0:T(8,128)} %copy-done.10, f32[4,768,64]{1,2,0:T(8,128)S(1)} %copy-done, f32[1,4,24,768]{3,2,1,0:T(8,128)} %param.26, f32[4,24,768]{2,1,0:T(8,128)S(1)} %copy-done.5, f32[1,4,24,768]{3,2,1,0:T(8,128)} %param.18), kind=kOutput, calls=%fused_computation.5 | convolution fusion | flops 56844288 | bytes 1990656 | tf_op jit(solution)/shard_map/mrk,mdk->mrd/dot_general | solution.py:40
  142.6 27.9 %all-gather.6.cloned.1.call-done = bf16[768,3072]{1,0:T(8,128)(2,1)} async-done(((bf16[24,3072]{1,0:T(8,128)(2,1)}), bf16[768,3072]{1,0:T(8,128)(2,1)}) %all-gather.6.cloned.1.call-update) | async-done | bytes 4718608 | tf_op jit(solution)/shard_map/all_gather | solution.py:66
  170.6 5.0 %copy.34 = bf16[4,768,768]{2,1,0:T(8,128)(2,1)} copy(bf16[4,768,768]{2,1,0:T(8,128)(2,1)} %all-gather.4.cloned.1.call-done) | data formatting | bytes 9437184
  175.6 2.2 %copy.35 = bf16[768,3072]{1,0:T(8,128)(2,1)} copy(bf16[768,3072]{1,0:T(8,128)(2,1)S(1)} %copy-done.2) | data formatting | bytes 9437184
  177.8 4.8 %copy.36 = bf16[3072,768]{1,0:T(8,128)(2,1)} copy(bf16[3072,768]{1,0:T(8,128)(2,1)} %bitcast.10) | data formatting | bytes 9437184
  (33 shorter events, 0.1 us)
Async XLA Ops:
  7.2 1.6 copy-start
  7.2 24.1 %copy-start.5 = (f32[4,24,768]{2,1,0:T(8,128)S(1)}, f32[4,24,768]{2,1,0:T(8,128)}, u32[]{:S(2)}) copy-start(f32[4,24,768]{2,1,0:T(8,128)} %param.22) | copy-start | bytes 884740
  7.2 26.8 %copy-start.4 = (f32[96,768]{1,0:T(8,128)S(1)}, f32[96,768]{1,0:T(8,128)}, u32[]{:S(2)}) copy-start(f32[96,768]{1,0:T(8,128)} %param.24) | copy-start | bytes 884740
  7.2 26.8 %copy-start.6 = (f32[768,64]{0,1:T(8,128)S(1)}, f32[768,64]{0,1:T(8,128)}, u32[]{:S(2)}) copy-start(f32[768,64]{0,1:T(8,128)} %param.35) | copy-start | bytes 589828
  7.2 25.5 %copy-start.3 = (f32[24,3072]{1,0:T(8,128)S(1)}, f32[24,3072]{1,0:T(8,128)}, u32[]{:S(2)}) copy-start(f32[24,3072]{1,0:T(8,128)} %param.23) | copy-start | bytes 884740
  7.2 25.5 %copy-start.1 = (f32[3072,64]{0,1:T(8,128)S(1)}, f32[3072,64]{0,1:T(8,128)}, u32[]{:S(2)}) copy-start(f32[3072,64]{0,1:T(8,128)} %param.34) | copy-start | bytes 2359300
  7.3 24.1 %copy-start.11 = (f32[4,24,768]{2,1,0:T(8,128)S(1)}, f32[4,24,768]{2,1,0:T(8,128)}, u32[]{:S(2)}) copy-start(f32[4,24,768]{2,1,0:T(8,128)} %param.29) | copy-start | bytes 884740
  7.3 25.4 %copy-start.12 = (f32[24,3072]{1,0:T(8,128)S(1)}, f32[24,3072]{1,0:T(8,128)}, u32[]{:S(2)}) copy-start(f32[24,3072]{1,0:T(8,128)} %param.30) | copy-start | bytes 884740
  7.3 135.4 %all-gather.4.cloned.1.call-start = ((), (), s32[]{:S(2)}) async-start(), calls=%async_computation.1 | async-start | bytes 4866048 | tf_op jit(solution)/shard_map/all_gather | solution.py:65
  10.7 25.5 %copy-start.10 = (f32[4,24,64]{2,1,0:T(8,128)}, f32[4,24,64]{2,1,0:T(8,128)S(1)}, u32[]{:S(2)}) copy-start(f32[4,24,64]{2,1,0:T(8,128)S(1)} %fusion.16) | copy-start | bytes 73732
  12.3 23.9 %copy-start.13 = (f32[96,64]{0,1:T(8,128)}, f32[96,64]{0,1:T(8,128)S(1)}, u32[]{:S(2)}) copy-start(f32[96,64]{0,1:T(8,128)S(1)} %fusion.18) | copy-start | bytes 73732
  32.6 137.9 %all-gather.6.cloned.1.call-start = ((), (), s32[]{:S(2)}) async-start(), calls=%async_computation.2 | async-start | bytes 4866048 | tf_op jit(solution)/shard_map/all_gather | solution.py:66
  39.0 11.7 %copy-start.14 = (f32[4,24]{1,0:T(4,128)S(1)}, f32[4,24]{1,0:T(4,128)}, u32[]{:S(2)}) copy-start(f32[4,24]{1,0:T(4,128)} %param.25) | copy-start | bytes 1156
  39.0 98.0 %copy-start.9 = (f32[1,96,768]{2,1,0:T(8,128)S(1)}, f32[1,96,768]{2,1,0:T(8,128)}, u32[]{:S(2)}) copy-start(f32[1,96,768]{2,1,0:T(8,128)} %param.28) | copy-start | bytes 884740
  39.0 100.2 %copy-start.7 = (f32[1,24,3072]{2,1,0:T(8,128)S(1)}, f32[1,24,3072]{2,1,0:T(8,128)}, u32[]{:S(2)}) copy-start(f32[1,24,3072]{2,1,0:T(8,128)} %param.27) | copy-start | bytes 884740
  39.0 100.2 %copy-start.8 = (f32[1,24,3072]{2,1,0:T(8,128)S(1)}, f32[1,24,3072]{2,1,0:T(8,128)}, u32[]{:S(2)}) copy-start(f32[1,24,3072]{2,1,0:T(8,128)} %param.19) | copy-start | bytes 884740
  39.0 103.7 %all-to-all-start = ((bf16[32,96,768]{2,1,0:T(8,128)(2,1)}), bf16[32,96,768]{2,1,0:T(8,128)(2,1)}, u32[]{:S(2)}, u32[]{:S(2)}) async-start(bf16[32,96,768]{2,1,0:T(8,128)(2,1)} %stack.2), calls=%async_computation | async-start | bytes 9437184 | tf_op jit(solution)/shard_map/all_to_all | solution.py:68
  170.6 5.0 %copy-start.2 = (bf16[768,3072]{1,0:T(8,128)(2,1)S(1)}, bf16[768,3072]{1,0:T(8,128)(2,1)}, u32[]{:S(2)}) copy-start(bf16[768,3072]{1,0:T(8,128)(2,1)} %all-gather.6.cloned.1.call-done) | copy-start | bytes 14155780
Sparse Core Ops, SparseCore 0:
  32.8 88.9 all-gather.3
  124.6 45.9 all-gather.5
